TPU v7x, 256 devices: a whole 4x4x8 slice. The times are simulated.
256 devices in a mesh: gx: 16 (over z, core), gy: 16 (over x, y).
Axes of the slice: x: 4, y: 4, z: 8, core: 2. Of those that a mesh axis runs over, the one named last changes fastest.
Arguments:
- forcing: float32 [4, 8, 4096, 2048], P(None, None, 'gx', 'gy'), may hold values from -150 to 150
- velocity: float32 [2, 4096, 2048], P(None, 'gx', 'gy'), may hold values from -0.6 to 0.6
- viscosity: float32 [4096, 2048], P('gx', 'gy'), may hold values from 0.05 to 0.25
- sound: float32 [4096, 2048], P('gx', 'gy'), may hold values from 0.4 to 1
- coupling: float32 [4, 4, 4096, 2048], P(None, None, 'gx', 'gy'), may hold values from -1.5 to 1.5
Outputs:
- basis: float32 [4, 8, 4096, 2048], P(None, None, 'gx', 'gy')
- factor: float32 [8, 8], replicated
All inputs are finite; a program needn't handle non-finite values.
Results may differ from a plain program's by a relative error of at most 0.000055.
Values sent between devices are 32-bit elements; how exact they have to be, the bound alone decides.
No kernel may reach another device: no remote copies, remote signals or barrier semaphores. Data moves between devices by JAX's collectives and lax.ppermute only.
A program may use at most 128 MiB of HBM per device.

v0:
```python
import jax
import jax.numpy as jnp
from jax import lax
from jax.sharding import PartitionSpec as P

STEP = 0.5


def with_halo(cells, sides, width):
    for axis, dim in sides:
        count = lax.axis_size(axis)
        ends = count - 1
        head = lax.slice_in_dim(cells, 0, width, axis=dim)
        tail = lax.slice_in_dim(cells, cells.shape[dim] - width, cells.shape[dim], axis=dim)
        cells = jnp.concatenate(
            [
                lax.ppermute(tail, axis, [(i, (i + 1) % count) for i in range(ends)]),
                cells,
                lax.ppermute(head, axis, [((i + 1) % count, i) for i in range(ends)]),
            ],
            axis=dim,
        )
    return cells


def tendency(padded, velocity, viscosity, sound, coupling):
    center = padded[:, :, 1:-1, 1:-1]
    east = padded[:, :, 2:, 1:-1]
    west = padded[:, :, :-2, 1:-1]
    north = padded[:, :, 1:-1, 2:]
    south = padded[:, :, 1:-1, :-2]
    grad_x = 0.5 * (east - west)
    grad_y = 0.5 * (north - south)
    laplace = east + west + north + south - 4.0 * center
    transport = viscosity * laplace - velocity[0] * grad_x - velocity[1] * grad_y
    divergence = grad_x[1] + grad_y[2]
    acoustic = jnp.stack(
        [-sound * divergence, -sound * grad_x[3], -sound * grad_y[3], -sound * divergence]
    )
    mixing = coupling[:, 0][:, None] * center[0][None]
    for inner in range(1, 4):
        mixing = mixing + coupling[:, inner][:, None] * center[inner][None]
    return transport + acoustic - mixing


def extend(state):
    return with_halo(state, (("gx", 2), ("gy", 3)), 1)


def local(forcing, velocity, viscosity, sound, coupling):
    first = tendency(extend(forcing), velocity, viscosity, sound, coupling) + forcing
    middle = forcing + STEP * first
    second = tendency(extend(middle), velocity, viscosity, sound, coupling) + forcing
    response = forcing + 0.5 * STEP * (first + second)
    rows_total = float(
        4 * forcing.shape[2] * forcing.shape[3] * lax.axis_size("gx") * lax.axis_size("gy")
    )
    local_gram = (
        jnp.einsum("vcxy,vdxy->cd", response, response, precision=lax.Precision.HIGHEST)
        / rows_total
    )
    lower = jnp.linalg.cholesky(lax.psum(local_gram, ("gx", "gy")))
    identity = jnp.eye(lower.shape[0], dtype=lower.dtype)
    inverse = lax.linalg.triangular_solve(lower, identity, left_side=True, lower=True)
    basis = jnp.einsum("cd,vdxy->vcxy", inverse, response, precision=lax.Precision.HIGHEST)
    return (basis, lower.T)


def solution(mesh):
    in_specs = (
        P(None, None, "gx", "gy"),
        P(None, "gx", "gy"),
        P("gx", "gy"),
        P("gx", "gy"),
        P(None, None, "gx", "gy"),
    )
    out_specs = (P(None, None, "gx", "gy"), P())
    return jax.shard_map(local, mesh=mesh, in_specs=in_specs, out_specs=out_specs, check_vma=False)
```

profile of v0, /device:TPU:1, one launch (start us, length us, event | category | flops | bytes accessed | tf_op | source)
XLA Modules:
  0.0 236.0 jit_solution(18305960756760041180)
XLA Ops:
  1.6 5.1 %collective-permute-start = (f32[4,8,1,128]{3,1,2,0:T(8,128)S(1)}, f32[4,8,1,128]{3,1,2,0:T(8,128)S(1)}, u32[]{:S(2)}, u32[]{:S(2)}) collective-permute-start(f32[4,8,1,128]{3,1,2,0:T(8,128)S(1)} %bitcast.57), channel_id=1, source_target_pairs={{16,0},{32,16},{48,32},{64,48},{80,64},{96,80},{112,96},{128,112},... | collective-permute-start | bytes 49160 | tf_op jit(solution)/shard_map/ppermute | solution.py:19
  6.8 2.1 collective-permute-start.1
  8.8 3.8 %slice_bitcast_fusion.7 = (f32[8,256,128]{2,1,0:T(8,128)}, f32[8,256,128]{2,1,0:T(8,128)S(1)}, f32[8,256,128]{2,1,0:T(8,128)}, f32[8,256,128]{2,1,0:T(8,128)}) fusion(f32[4,8,256,128]{3,2,1,0:T(8,128)} %param.5), kind=kLoop, calls=%fused_computation.51 | loop fusion | bytes 8388608 | tf_op jit(solution)/shard_map/mul | solution.py:40
  14.1 5.4 %copy.76 = f32[4,8,256,128]{2,1,3,0:T(8,128)} copy(f32[4,8,256,128]{3,2,1,0:T(8,128)} %param.5) | data formatting | bytes 8388608 | tf_op args[0]
  20.3 2.0 copy.50
  22.2 1.6 pad_maximum_fusion.19
  23.8 3.6 %collective-permute-start.3 = (f32[4,8,258,1]{2,1,3,0:T(8,128)}, f32[4,8,258,1]{2,1,3,0:T(8,128)}, u32[]{:S(2)}, u32[]{:S(2)}) collective-permute-start(f32[4,8,258,1]{2,1,3,0:T(8,128)} %get-tuple-element.16), channel_id=1, source_target_pairs={{0,1},{1,2},{2,3},{3,4},{4,5},{5,6},{6,7},{7,8},{8,9},{9,10},{10,1... | collective-permute-start | bytes 99080 | tf_op jit(solution)/shard_map/ppermute | solution.py:17
  31.4 2.6 %copy.64 = f32[8,256,128]{1,0,2:T(8,128)} copy(f32[8,256,128]{2,1,0:T(8,128)} %get-tuple-element.35) | data formatting | bytes 2097152 | tf_op jit(solution)/shard_map/mul | solution.py:42
  35.3 2.6 %copy.62 = f32[8,256,128]{1,0,2:T(8,128)} copy(f32[8,256,128]{2,1,0:T(8,128)} %get-tuple-element.34) | data formatting | bytes 2097152 | tf_op jit(solution)/shard_map/mul | solution.py:42
  37.9 2.0 copy.61
  39.9 2.7 %copy.60 = f32[8,256,128]{1,0,2:T(8,128)} copy(f32[8,256,128]{2,1,0:T(8,128)} %get-tuple-element.32) | data formatting | bytes 2097152 | tf_op jit(solution)/shard_map/mul | solution.py:40
  42.6 2.0 copy.59
  47.6 10.8 %fusion.8 = (f32[4,8,256,128]{2,1,3,0:T(8,128)S(1)}, f32[4,8,256,128]{2,1,3,0:T(8,128)S(1)}) fusion(f32[4,8,1,128]{2,1,3,0:T(8,128)S(1)} %copy.48, f32[4,8,256,128]{2,1,3,0:T(8,128)} %copy.76, f32[4,8,1,128]{2,1,3,0:T(8,128)} %copy.50, f32[4,8,258,1]{2,1,3,0:T(8,128)} %collective-permute-done.3, f32[4,8,258,1]{2,1,3,0:T(8,128)} %collective-permute-done.2), kind=kLoop, calls=%fused_computation.27 | loop fusion | flops 12582912 | bytes 12681728 | tf_op jit(solution)/shard_map/mul | solution.py:32
  58.4 1.9 slice_multiply_fusion.3
  62.4 11.5 %multiply_add_fusion = (f32[4,8,256,128]{2,1,3,0:T(8,128)S(1)}, f32[4,8,256,128]{2,1,3,0:T(8,128)}) fusion(f32[4,8,256,128]{2,1,3,0:T(8,128)S(1)} %copy-done.2, f32[8,256,128]{1,0,2:T(8,128)} %copy.66, f32[4,256,128]{1,2,0:T(8,128)S(1)} %copy.65, f32[8,256,128]{1,0,2:T(8,128)} %copy.64, f32[4,256,128]{1,2,0:T(8,128)S(1)} %copy.63, f32[8,256,128]{1,0,2:T(8,128)} %copy.62, ...), kind=kLoop, calls=%fused_computation.25 | loop fusion | flops 36700160 | bytes 22512128 | tf_op jit(solution)/shard_map/add | solution.py:52
  73.9 2.5 %fusion.18 = (f32[4,8,1,128]{2,1,3,0:T(8,128)S(1)}, f32[4,8,1,128]{2,1,3,0:T(8,128)}) fusion(f32[4,8,256,128]{2,1,3,0:T(8,128)S(1)} %get-tuple-element.8), kind=kLoop, calls=%fused_computation.74 | loop fusion | bytes 65536 | tf_op jit(solution)/shard_map/slice | solution.py:14
  76.6 2.2 copy.69
  78.8 1.9 collective-permute-start.4
  82.0 3.6 %collective-permute-start.5 = (f32[4,8,1,128]{3,1,2,0:T(8,128)}, f32[4,8,1,128]{3,1,2,0:T(8,128)}, u32[]{:S(2)}, u32[]{:S(2)}) collective-permute-start(f32[4,8,1,128]{3,1,2,0:T(8,128)} %copy.71), channel_id=1, source_target_pairs={{0,16},{16,32},{32,48},{48,64},{64,80},{80,96},{96,112},{112,128},... | collective-permute-start | bytes 49160 | tf_op jit(solution)/shard_map/ppermute | solution.py:17
  87.1 2.8 %copy.72 = f32[4,8,1,128]{2,1,3,0:T(8,128)} copy(f32[4,8,1,128]{3,1,2,0:T(8,128)} %collective-permute-done.5) | data formatting | bytes 32768 | tf_op jit(solution)/shard_map/ppermute | solution.py:17
  90.9 4.1 %collective-permute-start.7 = (f32[4,8,258,1]{2,1,3,0:T(8,128)S(1)}, f32[4,8,258,1]{2,1,3,0:T(8,128)S(1)}, u32[]{:S(2)}, u32[]{:S(2)}) collective-permute-start(f32[4,8,258,1]{2,1,3,0:T(8,128)S(1)} %get-tuple-element.12), channel_id=1, source_target_pairs={{0,1},{1,2},{2,3},{3,4},{4,5},{5,6},{6,7},{7,8},{8,9},{9,10},{10,1... | collective-permute-start | bytes 99080 | tf_op jit(solution)/shard_map/ppermute | solution.py:17
  95.0 1.6 collective-permute-start.6
  96.6 2.0 slice_bitcast_fusion.3
  98.6 2.0 collective-permute-done.6
  100.7 6.9 %fusion.10 = (f32[4,8,256,128]{2,1,3,0:T(8,128)}, f32[4,8,256,128]{2,1,3,0:T(8,128)}) fusion(f32[4,8,1,128]{2,1,3,0:T(8,128)S(1)} %copy.70, f32[4,8,256,128]{2,1,3,0:T(8,128)S(1)} %copy-done.1, f32[4,8,1,128]{2,1,3,0:T(8,128)S(1)} %copy-done.5, f32[4,8,258,1]{2,1,3,0:T(8,128)S(1)} %collective-permute-done.7, f32[4,8,258,1]{2,1,3,0:T(8,128)S(1)} %collective-permute-done.6), kind=kLoop, calls=%fused_computation.29 | loop fusion | flops 12582912 | bytes 12681728 | tf_op jit(solution)/shard_map/mul | solution.py:32
  107.6 4.0 %slice_multiply_fusion.1 = (f32[1,8,256,128]{2,1,3,0:T(8,128)S(1)}, f32[1,8,256,128]{2,1,3,0:T(8,128)}, f32[1,8,256,128]{2,1,3,0:T(8,128)}) fusion(f32[4,8,256,128]{2,1,3,0:T(8,128)} %get-tuple-element.10, f32[256,128]{0,1:T(8,128)S(1)} %copy-done.11, f32[4,8,256,128]{2,1,3,0:T(8,128)} %get-tuple-element.11), kind=kLoop, calls=%fused_computation.41 | loop fusion | flops 1048576 | bytes 7471104 | tf_op jit(solution)/shard_map/mul | solution.py:38
  111.8 11.4 %fusion.6 = f32[4,8,256,128]{2,1,3,0:T(8,128)} fusion(f32[4,8,256,128]{2,1,3,0:T(8,128)S(1)} %copy-done.3, f32[4,8,256,128]{2,1,3,0:T(8,128)S(1)} %copy-done.6, f32[1,8,256,128]{2,1,3,0:T(8,128)} %get-tuple-element.19, f32[1,8,256,128]{2,1,3,0:T(8,128)} %get-tuple-element.20, f32[1,8,256,128]{2,1,3,0:T(8,128)S(1)} %get-tuple-element.18, ...), kind=kLoop, calls=%fused_computation.24 | loop fusion | flops 37748736 | bytes 26706432 | tf_op jit(solution)/shard_map/add | solution.py:54
  123.2 5.5 %copy.80 = f32[4,8,256,128]{3,1,2,0:T(8,128)} copy(f32[4,8,256,128]{2,1,3,0:T(8,128)} %fusion.6) | data formatting | bytes 8388608 | tf_op jit(solution)/shard_map/add | solution.py:54
  128.7 12.6 %fusion.11 = f32[8,8]{0,1:T(8,128)S(1)} fusion(f32[4,8,256,128]{2,1,3,0:T(8,128)} %fusion.6), kind=kOutput, calls=%fused_computation.35 | convolution fusion | flops 100663360 | bytes 4194560 | tf_op jit(solution)/shard_map/vcxy,vdxy->cd/dot_general | solution.py:59
  141.2 83.0 %psum.7 = f32[8,8]{0,1:T(8,128)S(1)} all-reduce(f32[8,8]{0,1:T(8,128)S(1)} %fusion.11), channel_id=1, replica_groups=mesh['gx'=16,'gy'=16] {'gx','gy'}, use_global_device_ids=true, to_apply=%region_0.0 | all-reduce | flops 64 | bytes 512 | tf_op jit(solution)/shard_map/psum | solution.py:62
  227.2 5.3 %convolution_bitcast_fusion = f32[4,8,256,128]{3,1,2,0:T(8,128)S(1)} fusion(f32[4,8,256,128]{3,1,2,0:T(8,128)} %copy.80, f32[8,8,1,1]{1,0,3,2:T(8,128)S(1)} %convolution_bitcast_fusion.1), kind=kOutput, calls=%fused_computation.30 | convolution fusion | flops 100663296 | bytes 8388864 | tf_op jit(solution)/shard_map/cd,vdxy->vcxy/dot_general | solution.py:65
  232.5 2.8 %copy.81 = f32[4,8,256,128]{3,2,1,0:T(8,128)} copy(f32[4,8,256,128]{3,1,2,0:T(8,128)S(1)} %convolution_bitcast_fusion) | data formatting | bytes 8388608
  (58 shorter events, 20.9 us)
Async XLA Ops:
  1.6 17.9 %collective-permute-start = (f32[4,8,1,128]{3,1,2,0:T(8,128)S(1)}, f32[4,8,1,128]{3,1,2,0:T(8,128)S(1)}, u32[]{:S(2)}, u32[]{:S(2)}) collective-permute-start(f32[4,8,1,128]{3,1,2,0:T(8,128)S(1)} %bitcast.57), channel_id=1, source_target_pairs={{16,0},{32,16},{48,32},{64,48},{80,64},{96,80},{112,96},{128,112},... | collective-permute-start | bytes 49160 | tf_op jit(solution)/shard_map/ppermute | solution.py:19
  6.7 5.9 %copy-start.9 = (f32[4,4,256,128]{3,2,1,0:T(8,128)S(1)}, f32[4,4,256,128]{3,2,1,0:T(8,128)}, u32[]{:S(2)}) copy-start(f32[4,4,256,128]{3,2,1,0:T(8,128)} %param.9) | copy-start | bytes 6291460
  6.8 13.5 %collective-permute-start.1 = (f32[4,8,1,128]{3,1,2,0:T(8,128)S(1)}, f32[4,8,1,128]{3,1,2,0:T(8,128)S(1)}, u32[]{:S(2)}, u32[]{:S(2)}) collective-permute-start(f32[4,8,1,128]{3,1,2,0:T(8,128)S(1)} %bitcast.56), channel_id=1, source_target_pairs={{0,16},{16,32},{32,48},{48,64},{64,80},{80,96},{96,112},{112,128},... | collective-permute-start | bytes 49160 | tf_op jit(solution)/shard_map/ppermute | solution.py:17
  22.2 6.5 %copy-start.12 = (f32[2,256,128]{2,1,0:T(8,128)S(1)}, f32[2,256,128]{2,1,0:T(8,128)}, u32[]{:S(2)}) copy-start(f32[2,256,128]{2,1,0:T(8,128)} %param.6) | copy-start | bytes 786436
  23.8 23.7 %collective-permute-start.3 = (f32[4,8,258,1]{2,1,3,0:T(8,128)}, f32[4,8,258,1]{2,1,3,0:T(8,128)}, u32[]{:S(2)}, u32[]{:S(2)}) collective-permute-start(f32[4,8,258,1]{2,1,3,0:T(8,128)} %get-tuple-element.16), channel_id=1, source_target_pairs={{0,1},{1,2},{2,3},{3,4},{4,5},{5,6},{6,7},{7,8},{8,9},{9,10},{10,1... | collective-permute-start | bytes 99080 | tf_op jit(solution)/shard_map/ppermute | solution.py:17
  27.4 20.1 %collective-permute-start.2 = (f32[4,8,258,1]{2,1,3,0:T(8,128)}, f32[4,8,258,1]{2,1,3,0:T(8,128)}, u32[]{:S(2)}, u32[]{:S(2)}) collective-permute-start(f32[4,8,258,1]{2,1,3,0:T(8,128)} %get-tuple-element.17), channel_id=1, source_target_pairs={{1,0},{2,1},{3,2},{4,3},{5,4},{6,5},{7,6},{8,7},{9,8},{10,9},{11,1... | collective-permute-start | bytes 99080 | tf_op jit(solution)/shard_map/ppermute | solution.py:19
  47.5 10.9 %copy-start.10 = (f32[256,128]{0,1:T(8,128)S(1)}, f32[256,128]{0,1:T(8,128)}, u32[]{:S(2)}) copy-start(f32[256,128]{0,1:T(8,128)} %copy.58) | copy-start | bytes 393220
  58.4 3.3 %copy-start.2 = (f32[4,8,256,128]{2,1,3,0:T(8,128)S(1)}, f32[4,8,256,128]{2,1,3,0:T(8,128)}, u32[]{:S(2)}) copy-start(f32[4,8,256,128]{2,1,3,0:T(8,128)} %copy.76) | copy-start | bytes 12582916
  58.4 4.0 %copy-start.4 = (f32[4,8,1,128]{2,1,3,0:T(8,128)S(1)}, f32[4,8,1,128]{2,1,3,0:T(8,128)}, u32[]{:S(2)}) copy-start(f32[4,8,1,128]{2,1,3,0:T(8,128)} %copy.50) | copy-start | bytes 49156
  73.9 2.7 %copy-start = (f32[4,8,256,128]{2,1,3,0:T(8,128)}, f32[4,8,256,128]{2,1,3,0:T(8,128)S(1)}, u32[]{:S(2)}) copy-start(f32[4,8,256,128]{2,1,3,0:T(8,128)S(1)} %get-tuple-element.8) | copy-start | bytes 12582916
  78.8 6.8 %collective-permute-start.4 = (f32[4,8,1,128]{3,1,2,0:T(8,128)S(1)}, f32[4,8,1,128]{3,1,2,0:T(8,128)}, u32[]{:S(2)}, u32[]{:S(2)}) collective-permute-start(f32[4,8,1,128]{3,1,2,0:T(8,128)S(1)} %copy.69), channel_id=1, source_target_pairs={{16,0},{32,16},{48,32},{64,48},{80,64},{96,80},{112,96},{128,112},... | collective-permute-start | bytes 49160 | tf_op jit(solution)/shard_map/ppermute | solution.py:19
  82.0 5.1 %collective-permute-start.5 = (f32[4,8,1,128]{3,1,2,0:T(8,128)}, f32[4,8,1,128]{3,1,2,0:T(8,128)}, u32[]{:S(2)}, u32[]{:S(2)}) collective-permute-start(f32[4,8,1,128]{3,1,2,0:T(8,128)} %copy.71), channel_id=1, source_target_pairs={{0,16},{16,32},{32,48},{48,64},{64,80},{80,96},{96,112},{112,128},... | collective-permute-start | bytes 49160 | tf_op jit(solution)/shard_map/ppermute | solution.py:17
  89.8 6.8 %copy-start.1 = (f32[4,8,256,128]{2,1,3,0:T(8,128)S(1)}, f32[4,8,256,128]{2,1,3,0:T(8,128)}, u32[]{:S(2)}) copy-start(f32[4,8,256,128]{2,1,3,0:T(8,128)} %copy-done) | copy-start | bytes 12582916
  90.9 7.8 %collective-permute-start.7 = (f32[4,8,258,1]{2,1,3,0:T(8,128)S(1)}, f32[4,8,258,1]{2,1,3,0:T(8,128)S(1)}, u32[]{:S(2)}, u32[]{:S(2)}) collective-permute-start(f32[4,8,258,1]{2,1,3,0:T(8,128)S(1)} %get-tuple-element.12), channel_id=1, source_target_pairs={{0,1},{1,2},{2,3},{3,4},{4,5},{5,6},{6,7},{7,8},{8,9},{9,10},{10,1... | collective-permute-start | bytes 99080 | tf_op jit(solution)/shard_map/ppermute | solution.py:17
  95.0 5.7 %copy-start.5 = (f32[4,8,1,128]{2,1,3,0:T(8,128)S(1)}, f32[4,8,1,128]{2,1,3,0:T(8,128)}, u32[]{:S(2)}) copy-start(f32[4,8,1,128]{2,1,3,0:T(8,128)} %copy.72) | copy-start | bytes 49156
  95.0 5.7 %collective-permute-start.6 = (f32[4,8,258,1]{2,1,3,0:T(8,128)S(1)}, f32[4,8,258,1]{2,1,3,0:T(8,128)S(1)}, u32[]{:S(2)}, u32[]{:S(2)}) collective-permute-start(f32[4,8,258,1]{2,1,3,0:T(8,128)S(1)} %get-tuple-element.13), channel_id=1, source_target_pairs={{1,0},{2,1},{3,2},{4,3},{5,4},{6,5},{7,6},{8,7},{9,8},{10,9},{11,1... | collective-permute-start | bytes 99080 | tf_op jit(solution)/shard_map/ppermute | solution.py:19
  98.6 9.0 %copy-start.11 = (f32[256,128]{0,1:T(8,128)S(1)}, f32[256,128]{0,1:T(8,128)}, u32[]{:S(2)}) copy-start(f32[256,128]{0,1:T(8,128)} %copy.58) | copy-start | bytes 393220
  100.7 10.9 %copy-start.6 = (f32[4,8,256,128]{2,1,3,0:T(8,128)S(1)}, f32[4,8,256,128]{2,1,3,0:T(8,128)}, u32[]{:S(2)}) copy-start(f32[4,8,256,128]{2,1,3,0:T(8,128)} %get-tuple-element.9) | copy-start | bytes 12582916
  107.6 4.0 %copy-start.3 = (f32[4,8,256,128]{2,1,3,0:T(8,128)S(1)}, f32[4,8,256,128]{2,1,3,0:T(8,128)}, u32[]{:S(2)}) copy-start(f32[4,8,256,128]{2,1,3,0:T(8,128)} %copy.76) | copy-start | bytes 12582916
  107.6 4.0 %copy-start.7 = (f32[4,256,128]{1,2,0:T(8,128)S(1)}, f32[4,256,128]{1,2,0:T(8,128)}, u32[]{:S(2)}) copy-start(f32[4,256,128]{1,2,0:T(8,128)} %copy.61) | copy-start | bytes 1572868
  107.6 4.1 %copy-start.8 = (f32[4,256,128]{1,2,0:T(8,128)S(1)}, f32[4,256,128]{1,2,0:T(8,128)}, u32[]{:S(2)}) copy-start(f32[4,256,128]{1,2,0:T(8,128)} %copy.59) | copy-start | bytes 1572868
where the time goes:
time: 237 us; the launch traced here: 236 us
  blocking collectives  83 us (35%)
  local copies, waits for them, and re-layouts  55.8 us (24%)
  other arithmetic  52.7 us (22%)
  starting transfers between devices  23.3 us (10%)
  matrix products  18.1 us (8%)
    psum x1, blocking collectives, local(): lower = jnp.linalg.cholesky(lax.psum(local_gram, ('gx', 'gy')))  83 us
    mul x2, other arithmetic, tendency(): grad_x = 0.5 * (east - west)  17.8 us
    ppermute x4, starting transfers between devices, with_halo(): lax.ppermute(tail, axis, [(i, (i + 1) % count) for i in range(ends)])  13.4 us
    dot_general x1, matrix products, local(): jnp.einsum('vcxy,vdxy->cd', response, response, precision=lax.Precision.H...  12.6 us
    unnamed x30, local copies, waits for them, and re-layouts  12.3 us
    mul x5, local copies, waits for them, and re-layouts, tendency(): mixing = coupling[:, 0][:, None] * center[0][None]  12.1 us
    add x1, other arithmetic, local(): middle = forcing + STEP * first  11.5 us
    add x1, other arithmetic, local(): response = forcing + 0.5 * STEP * (first + second)  11.4 us
  transfers between devices with their start and end apart: 8, of which 1 were waited for; matrix products, arithmetic and copies ran while one was open for 15% of the time, Pallas kernels for 0%

commit v1 on v0

--- a/solution.py
+++ b/solution.py
@@ -4,6 +4,11 @@
 from jax.sharding import PartitionSpec as P
 
 STEP = 0.5
+
+
+def cover_sums_all(mat, ax_name):
+    raw_out = lax.all_gather(mat, ax_name)
+    return jnp.sum(raw_out, axis=0)
 
 
 def with_halo(cells, sides, width):
@@ -59,7 +64,7 @@
         jnp.einsum("vcxy,vdxy->cd", response, response, precision=lax.Precision.HIGHEST)
         / rows_total
     )
-    lower = jnp.linalg.cholesky(lax.psum(local_gram, ("gx", "gy")))
+    lower = jnp.linalg.cholesky(cover_sums_all(local_gram, ("gx", "gy")))
     identity = jnp.eye(lower.shape[0], dtype=lower.dtype)
     inverse = lax.linalg.triangular_solve(lower, identity, left_side=True, lower=True)
     basis = jnp.einsum("cd,vdxy->vcxy", inverse, response, precision=lax.Precision.HIGHEST)

time: 237 us -> 266 us (1.12)
  blocking collectives: 83 us -> 110 us
    all_gather x0 -> x1, blocking collectives: none -> 110 us  [cover_sums_all(): raw_out = lax.all_gather(mat, ax_name)]
    psum x1 -> x0, blocking collectives: 83 us -> none  [local(): lower = jnp.linalg.cholesky(lax.psum(local_gram, ('gx', 'gy')))]
  transfers between devices with their start and end apart: 8 -> 8, of which waited for: 1 -> 1; matrix products, arithmetic and copies ran while one was open for 15% -> 13% of each run, Pallas kernels for 0% -> 0%
where the time goes in v1:
time: 266 us; the launch traced here: 263 us
  blocking collectives  110 us (41%)
  local copies, waits for them, and re-layouts  55.8 us (21%)
  other arithmetic  53 us (20%)
  starting transfers between devices  23.3 us (9%)
  matrix products  18.7 us (7%)
    all_gather x1, blocking collectives, cover_sums_all(): raw_out = lax.all_gather(mat, ax_name)  110 us
    mul x2, other arithmetic, tendency(): grad_x = 0.5 * (east - west)  17.8 us
    ppermute x4, starting transfers between devices, with_halo(): lax.ppermute(tail, axis, [(i, (i + 1) % count) for i in range(ends)])  13.4 us
    dot_general x1, matrix products, local(): jnp.einsum('vcxy,vdxy->cd', response, response, precision=lax.Precision.H...  13.1 us
    unnamed x30, local copies, waits for them, and re-layouts  12.3 us
    mul x5, local copies, waits for them, and re-layouts, tendency(): mixing = coupling[:, 0][:, None] * center[0][None]  12.1 us
    add x1, other arithmetic, local(): middle = forcing + STEP * first  11.5 us
    add x1, other arithmetic, local(): response = forcing + 0.5 * STEP * (first + second)  11.4 us
  transfers between devices with their start and end apart: 8, of which 1 were waited for; matrix products, arithmetic and copies ran while one was open for 13% of the time, Pallas kernels for 0%

profile of v1, /device:TPU:1, one launch (start us, length us, event | category | flops | bytes accessed | tf_op | source)
XLA Modules:
  0.0 263.3 jit_solution(1248384867891236437)
XLA Ops:
  1.6 5.1 %collective-permute-start = (f32[4,8,1,128]{3,1,2,0:T(8,128)S(1)}, f32[4,8,1,128]{3,1,2,0:T(8,128)S(1)}, u32[]{:S(2)}, u32[]{:S(2)}) collective-permute-start(f32[4,8,1,128]{3,1,2,0:T(8,128)S(1)} %bitcast.61), channel_id=1, source_target_pairs={{16,0},{32,16},{48,32},{64,48},{80,64},{96,80},{112,96},{128,112},... | collective-permute-start | bytes 49160 | tf_op jit(solution)/shard_map/ppermute | solution.py:24
  6.8 2.1 collective-permute-start.1
  8.8 3.8 %slice_bitcast_fusion.7 = (f32[8,256,128]{2,1,0:T(8,128)}, f32[8,256,128]{2,1,0:T(8,128)S(1)}, f32[8,256,128]{2,1,0:T(8,128)}, f32[8,256,128]{2,1,0:T(8,128)}) fusion(f32[4,8,256,128]{3,2,1,0:T(8,128)} %param.5), kind=kLoop, calls=%fused_computation.52 | loop fusion | bytes 8388608 | tf_op jit(solution)/shard_map/mul | solution.py:45
  14.1 5.4 %copy.74 = f32[4,8,256,128]{2,1,3,0:T(8,128)} copy(f32[4,8,256,128]{3,2,1,0:T(8,128)} %param.5) | data formatting | bytes 8388608 | tf_op args[0]
  20.3 2.0 copy.48
  22.3 1.6 pad_maximum_fusion.19
  23.8 3.6 %collective-permute-start.3 = (f32[4,8,258,1]{2,1,3,0:T(8,128)}, f32[4,8,258,1]{2,1,3,0:T(8,128)}, u32[]{:S(2)}, u32[]{:S(2)}) collective-permute-start(f32[4,8,258,1]{2,1,3,0:T(8,128)} %get-tuple-element.16), channel_id=1, source_target_pairs={{0,1},{1,2},{2,3},{3,4},{4,5},{5,6},{6,7},{7,8},{8,9},{9,10},{10,1... | collective-permute-start | bytes 99080 | tf_op jit(solution)/shard_map/ppermute | solution.py:22
  31.4 2.6 copy.62
  35.3 2.6 copy.60
  37.9 2.0 copy.59
  39.9 2.7 %copy.58 = f32[8,256,128]{1,0,2:T(8,128)} copy(f32[8,256,128]{2,1,0:T(8,128)} %get-tuple-element.32) | data formatting | bytes 2097152 | tf_op jit(solution)/shard_map/mul | solution.py:45
  42.6 2.0 copy.57
  47.6 10.8 %fusion.8 = (f32[4,8,256,128]{2,1,3,0:T(8,128)S(1)}, f32[4,8,256,128]{2,1,3,0:T(8,128)S(1)}) fusion(f32[4,8,1,128]{2,1,3,0:T(8,128)S(1)} %copy.46, f32[4,8,256,128]{2,1,3,0:T(8,128)} %copy.74, f32[4,8,1,128]{2,1,3,0:T(8,128)} %copy.48, f32[4,8,258,1]{2,1,3,0:T(8,128)} %collective-permute-done.3, f32[4,8,258,1]{2,1,3,0:T(8,128)} %collective-permute-done.2), kind=kLoop, calls=%fused_computation.27 | loop fusion | flops 12582912 | bytes 12681728 | tf_op jit(solution)/shard_map/mul | solution.py:37
  58.4 1.9 slice_multiply_fusion.3
  62.4 11.5 %multiply_add_fusion = (f32[4,8,256,128]{2,1,3,0:T(8,128)S(1)}, f32[4,8,256,128]{2,1,3,0:T(8,128)}) fusion(f32[4,8,256,128]{2,1,3,0:T(8,128)S(1)} %copy-done.2, f32[8,256,128]{1,0,2:T(8,128)} %copy.64, f32[4,256,128]{1,2,0:T(8,128)S(1)} %copy.63, f32[8,256,128]{1,0,2:T(8,128)} %copy.62, f32[4,256,128]{1,2,0:T(8,128)S(1)} %copy.61, f32[8,256,128]{1,0,2:T(8,128)} %copy.60, ...), kind=kLoop, calls=%fused_computation.25 | loop fusion | flops 36700160 | bytes 22512128 | tf_op jit(solution)/shard_map/add | solution.py:57
  73.9 2.5 fusion.18
  76.6 2.2 copy.67
  78.8 1.9 collective-permute-start.4
  82.0 3.6 %collective-permute-start.5 = (f32[4,8,1,128]{3,1,2,0:T(8,128)}, f32[4,8,1,128]{3,1,2,0:T(8,128)}, u32[]{:S(2)}, u32[]{:S(2)}) collective-permute-start(f32[4,8,1,128]{3,1,2,0:T(8,128)} %copy.69), channel_id=1, source_target_pairs={{0,16},{16,32},{32,48},{48,64},{64,80},{80,96},{96,112},{112,128},... | collective-permute-start | bytes 49160 | tf_op jit(solution)/shard_map/ppermute | solution.py:22
  87.1 2.8 %copy.70 = f32[4,8,1,128]{2,1,3,0:T(8,128)} copy(f32[4,8,1,128]{3,1,2,0:T(8,128)} %collective-permute-done.5) | data formatting | bytes 32768 | tf_op jit(solution)/shard_map/ppermute | solution.py:22
  90.9 4.1 %collective-permute-start.7 = (f32[4,8,258,1]{2,1,3,0:T(8,128)S(1)}, f32[4,8,258,1]{2,1,3,0:T(8,128)S(1)}, u32[]{:S(2)}, u32[]{:S(2)}) collective-permute-start(f32[4,8,258,1]{2,1,3,0:T(8,128)S(1)} %get-tuple-element.12), channel_id=1, source_target_pairs={{0,1},{1,2},{2,3},{3,4},{4,5},{5,6},{6,7},{7,8},{8,9},{9,10},{10,1... | collective-permute-start | bytes 99080 | tf_op jit(solution)/shard_map/ppermute | solution.py:22
  95.0 1.6 collective-permute-start.6
  96.6 2.0 slice_bitcast_fusion.3
  98.7 2.0 collective-permute-done.6
  100.7 6.9 %fusion.10 = (f32[4,8,256,128]{2,1,3,0:T(8,128)}, f32[4,8,256,128]{2,1,3,0:T(8,128)}) fusion(f32[4,8,1,128]{2,1,3,0:T(8,128)S(1)} %copy.68, f32[4,8,256,128]{2,1,3,0:T(8,128)S(1)} %copy-done.1, f32[4,8,1,128]{2,1,3,0:T(8,128)S(1)} %copy-done.5, f32[4,8,258,1]{2,1,3,0:T(8,128)S(1)} %collective-permute-done.7, f32[4,8,258,1]{2,1,3,0:T(8,128)S(1)} %collective-permute-done.6), kind=kLoop, calls=%fused_computation.29 | loop fusion | flops 12582912 | bytes 12681728 | tf_op jit(solution)/shard_map/mul | solution.py:37
  107.6 4.0 %slice_multiply_fusion.1 = (f32[1,8,256,128]{2,1,3,0:T(8,128)S(1)}, f32[1,8,256,128]{2,1,3,0:T(8,128)}, f32[1,8,256,128]{2,1,3,0:T(8,128)}) fusion(f32[4,8,256,128]{2,1,3,0:T(8,128)} %get-tuple-element.10, f32[256,128]{0,1:T(8,128)S(1)} %copy-done.11, f32[4,8,256,128]{2,1,3,0:T(8,128)} %get-tuple-element.11), kind=kLoop, calls=%fused_computation.41 | loop fusion | flops 1048576 | bytes 7471104 | tf_op jit(solution)/shard_map/mul | solution.py:43
  111.8 11.4 %fusion.6 = f32[4,8,256,128]{2,1,3,0:T(8,128)} fusion(f32[4,8,256,128]{2,1,3,0:T(8,128)S(1)} %copy-done.3, f32[4,8,256,128]{2,1,3,0:T(8,128)S(1)} %copy-done.6, f32[1,8,256,128]{2,1,3,0:T(8,128)} %get-tuple-element.19, f32[1,8,256,128]{2,1,3,0:T(8,128)} %get-tuple-element.20, f32[1,8,256,128]{2,1,3,0:T(8,128)S(1)} %get-tuple-element.18, ...), kind=kLoop, calls=%fused_computation.24 | loop fusion | flops 37748736 | bytes 26706432 | tf_op jit(solution)/shard_map/add | solution.py:59
  123.2 5.5 %copy.77 = f32[4,8,256,128]{3,1,2,0:T(8,128)} copy(f32[4,8,256,128]{2,1,3,0:T(8,128)} %fusion.6) | data formatting | bytes 8388608 | tf_op jit(solution)/shard_map/add | solution.py:59
  128.7 13.1 %fusion.11 = f32[8,8]{1,0:T(8,128)S(1)} fusion(f32[4,8,256,128]{2,1,3,0:T(8,128)} %fusion.6), kind=kOutput, calls=%fused_computation.35 | convolution fusion | flops 100663360 | bytes 4194560 | tf_op jit(solution)/shard_map/vcxy,vdxy->cd/dot_general | solution.py:64
  141.8 109.6 %all-gather = f32[2048,8]{1,0:T(8,128)S(1)} all-gather(f32[8,8]{1,0:T(8,128)S(1)} %fusion.11), channel_id=2, replica_groups=mesh['gx'=16,'gy'=16] {'gx','gy'}, dimensions={0}, use_global_device_ids=true | all-gather | bytes 65792 | tf_op jit(solution)/shard_map/all_gather | solution.py:10
  254.6 5.3 %convolution_bitcast_fusion = f32[4,8,256,128]{3,1,2,0:T(8,128)S(1)} fusion(f32[4,8,256,128]{3,1,2,0:T(8,128)} %copy.77, f32[8,8,1,1]{1,0,3,2:T(8,128)S(1)} %convolution_bitcast_fusion.1), kind=kOutput, calls=%fused_computation.30 | convolution fusion | flops 100663296 | bytes 8388864 | tf_op jit(solution)/shard_map/cd,vdxy->vcxy/dot_general | solution.py:70
  259.9 2.8 %copy.78 = f32[4,8,256,128]{3,2,1,0:T(8,128)} copy(f32[4,8,256,128]{3,1,2,0:T(8,128)S(1)} %convolution_bitcast_fusion) | data formatting | bytes 8388608
  (59 shorter events, 21.2 us)
Async XLA Ops:
  1.6 17.9 %collective-permute-start = (f32[4,8,1,128]{3,1,2,0:T(8,128)S(1)}, f32[4,8,1,128]{3,1,2,0:T(8,128)S(1)}, u32[]{:S(2)}, u32[]{:S(2)}) collective-permute-start(f32[4,8,1,128]{3,1,2,0:T(8,128)S(1)} %bitcast.61), channel_id=1, source_target_pairs={{16,0},{32,16},{48,32},{64,48},{80,64},{96,80},{112,96},{128,112},... | collective-permute-start | bytes 49160 | tf_op jit(solution)/shard_map/ppermute | solution.py:24
  6.7 5.9 %copy-start.9 = (f32[4,4,256,128]{3,2,1,0:T(8,128)S(1)}, f32[4,4,256,128]{3,2,1,0:T(8,128)}, u32[]{:S(2)}) copy-start(f32[4,4,256,128]{3,2,1,0:T(8,128)} %param.9) | copy-start | bytes 6291460
  6.8 13.5 %collective-permute-start.1 = (f32[4,8,1,128]{3,1,2,0:T(8,128)S(1)}, f32[4,8,1,128]{3,1,2,0:T(8,128)S(1)}, u32[]{:S(2)}, u32[]{:S(2)}) collective-permute-start(f32[4,8,1,128]{3,1,2,0:T(8,128)S(1)} %bitcast.60), channel_id=1, source_target_pairs={{0,16},{16,32},{32,48},{48,64},{64,80},{80,96},{96,112},{112,128},... | collective-permute-start | bytes 49160 | tf_op jit(solution)/shard_map/ppermute | solution.py:22
  22.3 6.5 %copy-start.12 = (f32[2,256,128]{2,1,0:T(8,128)S(1)}, f32[2,256,128]{2,1,0:T(8,128)}, u32[]{:S(2)}) copy-start(f32[2,256,128]{2,1,0:T(8,128)} %param.6) | copy-start | bytes 786436
  23.8 23.7 %collective-permute-start.3 = (f32[4,8,258,1]{2,1,3,0:T(8,128)}, f32[4,8,258,1]{2,1,3,0:T(8,128)}, u32[]{:S(2)}, u32[]{:S(2)}) collective-permute-start(f32[4,8,258,1]{2,1,3,0:T(8,128)} %get-tuple-element.16), channel_id=1, source_target_pairs={{0,1},{1,2},{2,3},{3,4},{4,5},{5,6},{6,7},{7,8},{8,9},{9,10},{10,1... | collective-permute-start | bytes 99080 | tf_op jit(solution)/shard_map/ppermute | solution.py:22
  27.4 20.1 %collective-permute-start.2 = (f32[4,8,258,1]{2,1,3,0:T(8,128)}, f32[4,8,258,1]{2,1,3,0:T(8,128)}, u32[]{:S(2)}, u32[]{:S(2)}) collective-permute-start(f32[4,8,258,1]{2,1,3,0:T(8,128)} %get-tuple-element.17), channel_id=1, source_target_pairs={{1,0},{2,1},{3,2},{4,3},{5,4},{6,5},{7,6},{8,7},{9,8},{10,9},{11,1... | collective-permute-start | bytes 99080 | tf_op jit(solution)/shard_map/ppermute | solution.py:24
  47.5 10.9 %copy-start.10 = (f32[256,128]{0,1:T(8,128)S(1)}, f32[256,128]{0,1:T(8,128)}, u32[]{:S(2)}) copy-start(f32[256,128]{0,1:T(8,128)} %copy.56) | copy-start | bytes 393220
  58.4 3.3 %copy-start.2 = (f32[4,8,256,128]{2,1,3,0:T(8,128)S(1)}, f32[4,8,256,128]{2,1,3,0:T(8,128)}, u32[]{:S(2)}) copy-start(f32[4,8,256,128]{2,1,3,0:T(8,128)} %copy.74) | copy-start | bytes 12582916
  58.4 4.0 %copy-start.4 = (f32[4,8,1,128]{2,1,3,0:T(8,128)S(1)}, f32[4,8,1,128]{2,1,3,0:T(8,128)}, u32[]{:S(2)}) copy-start(f32[4,8,1,128]{2,1,3,0:T(8,128)} %copy.48) | copy-start | bytes 49156
  73.9 2.7 %copy-start = (f32[4,8,256,128]{2,1,3,0:T(8,128)}, f32[4,8,256,128]{2,1,3,0:T(8,128)S(1)}, u32[]{:S(2)}) copy-start(f32[4,8,256,128]{2,1,3,0:T(8,128)S(1)} %get-tuple-element.8) | copy-start | bytes 12582916
  78.8 6.8 %collective-permute-start.4 = (f32[4,8,1,128]{3,1,2,0:T(8,128)S(1)}, f32[4,8,1,128]{3,1,2,0:T(8,128)}, u32[]{:S(2)}, u32[]{:S(2)}) collective-permute-start(f32[4,8,1,128]{3,1,2,0:T(8,128)S(1)} %copy.67), channel_id=1, source_target_pairs={{16,0},{32,16},{48,32},{64,48},{80,64},{96,80},{112,96},{128,112},... | collective-permute-start | bytes 49160 | tf_op jit(solution)/shard_map/ppermute | solution.py:24
  82.0 5.1 %collective-permute-start.5 = (f32[4,8,1,128]{3,1,2,0:T(8,128)}, f32[4,8,1,128]{3,1,2,0:T(8,128)}, u32[]{:S(2)}, u32[]{:S(2)}) collective-permute-start(f32[4,8,1,128]{3,1,2,0:T(8,128)} %copy.69), channel_id=1, source_target_pairs={{0,16},{16,32},{32,48},{48,64},{64,80},{80,96},{96,112},{112,128},... | collective-permute-start | bytes 49160 | tf_op jit(solution)/shard_map/ppermute | solution.py:22
  89.8 6.8 %copy-start.1 = (f32[4,8,256,128]{2,1,3,0:T(8,128)S(1)}, f32[4,8,256,128]{2,1,3,0:T(8,128)}, u32[]{:S(2)}) copy-start(f32[4,8,256,128]{2,1,3,0:T(8,128)} %copy-done) | copy-start | bytes 12582916
  90.9 7.8 %collective-permute-start.7 = (f32[4,8,258,1]{2,1,3,0:T(8,128)S(1)}, f32[4,8,258,1]{2,1,3,0:T(8,128)S(1)}, u32[]{:S(2)}, u32[]{:S(2)}) collective-permute-start(f32[4,8,258,1]{2,1,3,0:T(8,128)S(1)} %get-tuple-element.12), channel_id=1, source_target_pairs={{0,1},{1,2},{2,3},{3,4},{4,5},{5,6},{6,7},{7,8},{8,9},{9,10},{10,1... | collective-permute-start | bytes 99080 | tf_op jit(solution)/shard_map/ppermute | solution.py:22
  95.0 5.7 %copy-start.5 = (f32[4,8,1,128]{2,1,3,0:T(8,128)S(1)}, f32[4,8,1,128]{2,1,3,0:T(8,128)}, u32[]{:S(2)}) copy-start(f32[4,8,1,128]{2,1,3,0:T(8,128)} %copy.70) | copy-start | bytes 49156
  95.0 5.7 %collective-permute-start.6 = (f32[4,8,258,1]{2,1,3,0:T(8,128)S(1)}, f32[4,8,258,1]{2,1,3,0:T(8,128)S(1)}, u32[]{:S(2)}, u32[]{:S(2)}) collective-permute-start(f32[4,8,258,1]{2,1,3,0:T(8,128)S(1)} %get-tuple-element.13), channel_id=1, source_target_pairs={{1,0},{2,1},{3,2},{4,3},{5,4},{6,5},{7,6},{8,7},{9,8},{10,9},{11,1... | collective-permute-start | bytes 99080 | tf_op jit(solution)/shard_map/ppermute | solution.py:24
  98.6 9.0 %copy-start.11 = (f32[256,128]{0,1:T(8,128)S(1)}, f32[256,128]{0,1:T(8,128)}, u32[]{:S(2)}) copy-start(f32[256,128]{0,1:T(8,128)} %copy.56) | copy-start | bytes 393220
  100.7 10.9 %copy-start.6 = (f32[4,8,256,128]{2,1,3,0:T(8,128)S(1)}, f32[4,8,256,128]{2,1,3,0:T(8,128)}, u32[]{:S(2)}) copy-start(f32[4,8,256,128]{2,1,3,0:T(8,128)} %get-tuple-element.9) | copy-start | bytes 12582916
  107.6 4.0 %copy-start.3 = (f32[4,8,256,128]{2,1,3,0:T(8,128)S(1)}, f32[4,8,256,128]{2,1,3,0:T(8,128)}, u32[]{:S(2)}) copy-start(f32[4,8,256,128]{2,1,3,0:T(8,128)} %copy.74) | copy-start | bytes 12582916
  107.6 4.0 %copy-start.7 = (f32[4,256,128]{1,2,0:T(8,128)S(1)}, f32[4,256,128]{1,2,0:T(8,128)}, u32[]{:S(2)}) copy-start(f32[4,256,128]{1,2,0:T(8,128)} %copy.59) | copy-start | bytes 1572868
  107.6 4.1 %copy-start.8 = (f32[4,256,128]{1,2,0:T(8,128)S(1)}, f32[4,256,128]{1,2,0:T(8,128)}, u32[]{:S(2)}) copy-start(f32[4,256,128]{1,2,0:T(8,128)} %copy.57) | copy-start | bytes 1572868
